TPU v7x, 32 devices: a whole 2x2x4 slice. The times are simulated.
32 devices in a mesh: layer: 2 (over x), gx: 8 (over z, core), gy: 2 (over y).
Axes of the slice: x: 2, y: 2, z: 4, core: 2. Of those that a mesh axis runs over, the one named last changes fastest.
Arguments:
- prev_vec: float32 [2, 16, 8, 32, 128], P('layer', 'gx', 'gy'), may hold values from -6 to 6
- cur_vec: float32 [2, 16, 8, 32, 128], P('layer', 'gx', 'gy'), may hold values from -6 to 6
- displace: float32 [2, 16, 8, 2, 128], P('layer', 'gx', 'gy'), may hold values from -0.15 to 0.15
- potential: float32 [2, 16, 8, 128], P('layer', 'gx', 'gy'), may hold values from -1.5 to 1.5
Outputs:
- first_term: float32 [2, 16, 8, 32, 128], P('layer', 'gx', 'gy')
- second_term: float32 [2, 16, 8, 32, 128], P('layer', 'gx', 'gy')
All inputs are finite; a program needn't handle non-finite values.
Results may differ from a plain program's by a relative error of at most 0.0003.
Values sent between devices are 32-bit elements; how exact they have to be, the bound alone decides.
No kernel may reach another device: no remote copies, remote signals or barrier semaphores. Data moves between devices by JAX's collectives and lax.ppermute only.
A program may use at most 64 MiB of HBM per device.

v0:
```python
import math

import jax
import jax.numpy as jnp
import numpy as np
from jax import lax
from jax.sharding import PartitionSpec as P

PATCH_X = 14
PATCH_Y = 4


v_pi = -2.7
v_sigma = 0.48
decay_len = 0.319
layer_gap = 3.35 / 1.42
cut_radius = 3.5
hop_scale = 12.0
twist_angle = 1.05 * math.pi / 180.0
root_three = math.sqrt(3.0)
cell_w = 4.0 * root_three
cell_h = 24.0
sigma_gain = v_sigma * math.exp((layer_gap - 1.0) / decay_len)
HI = lax.Precision.HIGHEST
OFFSETS = [(a, b) for a in (-1, 0, 1) for b in (-1, 0, 1)]


def _base_np():
    orbital = np.arange(128)
    sub = orbital % 4
    cell = orbital // 4
    inner_x = np.where((sub == 1) | (sub == 2), root_three / 2.0, 0.0)
    inner_y = np.select([sub == 1, sub == 2, sub == 3], [0.5, 1.5, 2.0], 0.0)
    return np.stack([(cell // 8) * root_three + inner_x - cell_w / 2.0, (cell % 8) * 3.0 + inner_y - cell_h / 2.0])


def _reach_sets():
    base = _base_np()
    c, s = math.cos(twist_angle), math.sin(twist_angle)
    rot = np.array([[c, -s], [s, c]])
    margin = 0.5
    plane_r = cut_radius + margin
    inter_r = math.sqrt(cut_radius**2 - layer_gap**2) + margin
    twists = [
        np.array([[cell_w * (i - (PATCH_X - 1) / 2.0)], [cell_h * (j - (PATCH_Y - 1) / 2.0)]])
        for i in range(PATCH_X)
        for j in range(PATCH_Y)
    ]
    sets = {}
    for a, b in OFFSETS:
        shift = np.array([[a * cell_w], [b * cell_h]])
        gap = base[:, :, None] - base[:, None, :] - shift[:, :, None]
        mask = np.sqrt((gap**2).sum(0)) < plane_r
        for e in twists:
            turned = rot @ base + (rot - np.eye(2)) @ e
            for own, near in ((base, turned), (turned, base)):
                gap = own[:, :, None] - near[:, None, :] - shift[:, :, None]
                mask |= np.sqrt((gap**2).sum(0)) < inter_r
        sets[(a, b)] = (np.nonzero(mask.any(1))[0], np.nonzero(mask.any(0))[0])
    return sets


REACH = _reach_sets()


def _one_hot(idx):
    table = np.zeros((128, len(idx)), np.float32)
    table[idx, np.arange(len(idx))] = 1.0
    return table


def pick(x, idx):
    if len(idx) == x.shape[-1]:
        return x
    if np.all(np.diff(idx) == 1):
        return x[..., idx[0] : idx[0] + len(idx)]
    return jnp.einsum("...q,qk->...k", x, _one_hot(idx), precision=HI)


def extended_2(value, sides, width):
    for axis, dim in sides:
        devices, length = (lax.axis_size(axis), value.shape[dim])
        up = [(i, (i + 1) % devices) for i in range(devices)]
        down = [(j, i) for i, j in up]
        last = lax.slice_in_dim(value, length - width, length, axis=dim)
        first = lax.slice_in_dim(value, 0, width, axis=dim)
        before = lax.ppermute(last, axis, up)
        after = lax.ppermute(first, axis, down)
        value = jnp.concatenate([before, value, after], axis=dim)
    return value


def partner_2(value, axis, distance):
    return lax.ppermute(value, axis, [(i, i ^ 1 << distance) for i in range(lax.axis_size(axis))])


def lattice(cos_vals, sin_vals):
    base = jnp.asarray(_base_np(), jnp.float32)
    rot_x = cos_vals[:, None] * base[0] - sin_vals[:, None] * base[1]
    rot_y = sin_vals[:, None] * base[0] + cos_vals[:, None] * base[1]
    return jnp.stack([rot_x, rot_y], axis=1)


def twist_offsets(cos_vals, sin_vals, row_ids, col_ids):
    along_x = cell_w * ((row_ids % PATCH_X).astype(jnp.float32) - (PATCH_X - 1) / 2.0)
    along_y = cell_h * ((col_ids % PATCH_Y).astype(jnp.float32) - (PATCH_Y - 1) / 2.0)
    cos_less = (cos_vals - 1.0)[:, None, None]
    sin_cast = sin_vals[:, None, None]
    shift_x = cos_less * along_x[None, :, None] - sin_cast * along_y[None, None, :]
    shift_y = sin_cast * along_x[None, :, None] + cos_less * along_y[None, None, :]
    return jnp.stack([shift_x, shift_y], axis=-1)[..., None]


def taper(dist_sq):
    scaled = dist_sq / (cut_radius * cut_radius)
    return jnp.maximum(1.0 - scaled * scaled, 0.0)


def plane_block(own_pos, near_pos, shift_x, shift_y, self_rows):
    delta_x = own_pos[..., 0, :, None] - near_pos[..., 0, None, :] - shift_x
    delta_y = own_pos[..., 1, :, None] - near_pos[..., 1, None, :] - shift_y
    dist_sq = delta_x * delta_x + delta_y * delta_y
    spread = jnp.sqrt(dist_sq)
    hopping = v_pi * jnp.exp(-(spread - 1.0) / decay_len) * taper(dist_sq)
    if self_rows:
        orbital = jnp.arange(128, dtype=jnp.int32)
        hopping = jnp.where(orbital[:, None] == orbital[None, :], 0.0, hopping)
    return hopping


def inter_block(own_pos, near_pos, shift_x, shift_y):
    delta_x = own_pos[..., 0, :, None] - near_pos[..., 0, None, :] - shift_x
    delta_y = own_pos[..., 1, :, None] - near_pos[..., 1, None, :] - shift_y
    dist_sq = delta_x * delta_x + delta_y * delta_y + layer_gap * layer_gap
    spread = jnp.sqrt(dist_sq)
    cosine_sq = layer_gap * layer_gap / dist_sq
    decay = jnp.exp(-(spread - 1.0) / decay_len)
    bonds = decay * (v_pi * (1.0 - cosine_sq) + sigma_gain * cosine_sq)
    return bonds * taper(dist_sq)


def body(prev_vec, cur_vec, displace, potential):
    layer_id = lax.axis_index("layer")
    tile_x = displace.shape[1]
    tile_y = displace.shape[2]
    cos_twist = math.cos(twist_angle)
    sin_twist = math.sin(twist_angle)
    partner = partner_2(displace, "layer", 0)
    both_disp = jnp.concatenate([displace, partner], axis=0)
    layer_up = layer_id == 1
    cos_vals = jnp.stack(
        [jnp.where(layer_up, cos_twist, 1.0), jnp.where(layer_up, 1.0, cos_twist)]
    ).astype(jnp.float32)
    sin_vals = jnp.stack(
        [jnp.where(layer_up, sin_twist, 0.0), jnp.where(layer_up, 0.0, sin_twist)]
    ).astype(jnp.float32)
    ext_disp = extended_2(both_disp, (("gx", 1), ("gy", 2)), 1)
    places = ext_disp + lattice(cos_vals, sin_vals)[:, None, None]
    row_count = tile_x * lax.axis_size("gx")
    col_count = tile_y * lax.axis_size("gy")
    row_ids = (
        lax.axis_index("gx") * tile_x + jnp.arange(tile_x + 2, dtype=jnp.int32) - 1 + row_count
    ) % row_count
    col_ids = (
        lax.axis_index("gy") * tile_y + jnp.arange(tile_y + 2, dtype=jnp.int32) - 1 + col_count
    ) % col_count
    twisted = places + twist_offsets(cos_vals, sin_vals, row_ids, col_ids)

    def own_view(value, a, b):
        return value[:, 1 + a : 1 + a + tile_x, 1 + b : 1 + b + tile_y]

    own_pos = own_view(places[:1], 0, 0)[0]
    own_twist = own_view(twisted[:1], 0, 0)[0]
    cos_own = cos_vals[0]
    sin_own = sin_vals[0]
    blocks = []
    for a, b in OFFSETS:
        rows, cols = REACH[(a, b)]
        shift_x = cos_own * (a * cell_w) - sin_own * (b * cell_h)
        shift_y = sin_own * (a * cell_w) + cos_own * (b * cell_h)
        near_pos = pick(own_view(places[:1], a, b)[0], cols)
        near_twist = pick(own_view(twisted[1:], a, b)[0], cols)
        plane = plane_block(pick(own_pos, rows), near_pos, shift_x, shift_y, a == 0 and b == 0)
        inter = inter_block(pick(own_twist, rows), near_twist, a * cell_w, b * cell_h)
        blocks.append((plane, inter))

    spread_rows = np.concatenate([REACH[o][0] for o in OFFSETS if len(REACH[o][0]) < 128])
    scatter = np.zeros((len(spread_rows), 128), np.float32)
    scatter[np.arange(len(spread_rows)), spread_rows] = 1.0

    def hop_terms(vectors):
        stacked = jnp.concatenate([vectors, partner_2(vectors, "layer", 0)], axis=0)
        extended = extended_2(stacked, (("gx", 1), ("gy", 2)), 1)
        full = potential[0][..., None, :] * vectors[0]
        parts = []
        for (a, b), (plane, inter) in zip(OFFSETS, blocks):
            rows, cols = REACH[(a, b)]
            near = pick(own_view(extended, a, b), cols)
            summed = jnp.einsum("xycq,xypq->xycp", near[0], plane, precision=HI)
            summed = summed + jnp.einsum("xycq,xypq->xycp", near[1], inter, precision=HI)
            if len(rows) == 128:
                full = full + summed
            else:
                parts.append(summed)
        full = full + jnp.einsum(
            "xycp,pn->xycn", jnp.concatenate(parts, axis=-1), scatter, precision=HI
        )
        return (full / hop_scale)[None]

    first_term = 2.0 * hop_terms(cur_vec) - prev_vec
    second_term = 2.0 * hop_terms(first_term) - cur_vec
    return (first_term, second_term)


def solution(mesh):
    in_specs = (
        P("layer", "gx", "gy", None, None),
        P("layer", "gx", "gy", None, None),
        P("layer", "gx", "gy", None, None),
        P("layer", "gx", "gy", None),
    )
    out_specs = (P("layer", "gx", "gy", None, None), P("layer", "gx", "gy", None, None))
    return jax.shard_map(body, mesh=mesh, in_specs=in_specs, out_specs=out_specs, check_vma=False)
```

profile of v0, /device:TPU:0, one launch (start us, length us, event | category | flops | bytes accessed | tf_op | source)
XLA Modules:
  0.0 89.8 jit_solution(1515343790084411661)
XLA Ops:
  0.6 0.7 fusion.396
  1.3 3.0 %collective-permute-start = (f32[1,2,4,2,128]{4,2,3,1,0:T(4,128)S(1)}, f32[1,2,4,2,128]{4,2,3,1,0:T(4,128)S(1)}, u32[]{:S(2)}, u32[]{:S(2)}) collective-permute-start(f32[1,2,4,2,128]{4,2,3,1,0:T(4,128)S(1)} %get-tuple-element.95), channel_id=1, source_target_pairs={{0,16},{16,0},{1,17},{17,1},{2,18},{18,2},{3,19},{19,3},{4,20},{20... | collective-permute-start | bytes 24584 | tf_op jit(solution)/shard_map/ppermute | solution.py:94
  4.3 0.9 %constant_dynamic-update-slice_fusion.3 = f32[2,2,4,32,128]{4,3,2,1,0:T(8,128)S(1)} fusion(f32[1,2,4,32,128]{4,3,2,1,0:T(8,128)} %param.44), kind=kLoop, calls=%fused_computation.152 | loop fusion | bytes 262144
  5.6 0.7 copy-done.9
  6.6 3.5 %collective-permute-start.2 = (f32[2,1,4,2,128]{4,2,3,1,0:T(4,128)S(1)}, f32[2,1,4,2,128]{4,2,3,1,0:T(4,128)S(1)}, u32[]{:S(2)}, u32[]{:S(2)}) collective-permute-start(f32[2,1,4,2,128]{4,2,3,1,0:T(4,128)S(1)} %get-tuple-element.24), channel_id=1, source_target_pairs={{2,0},{4,2},{6,4},{8,6},{10,8},{12,10},{14,12},{0,14},{3,1},{5,3},... | collective-permute-start | bytes 24584 | tf_op jit(solution)/shard_map/ppermute | solution.py:88
  10.1 1.3 %collective-permute-done.1 = f32[2,1,4,2,128]{4,2,3,1,0:T(4,128)S(1)} collective-permute-done((f32[2,1,4,2,128]{4,2,3,1,0:T(4,128)S(1)}, f32[2,1,4,2,128]{4,2,3,1,0:T(4,128)S(1)}, u32[]{:S(2)}, u32[]{:S(2)}) %collective-permute-start.1) | collective-permute-done | bytes 8224 | tf_op jit(solution)/shard_map/ppermute | solution.py:87
  11.5 2.1 %collective-permute-start.3 = (f32[2,4,1,2,128]{4,2,3,1,0:T(1,128)S(1)}, f32[2,4,1,2,128]{4,2,3,1,0:T(1,128)S(1)}, u32[]{:S(2)}, u32[]{:S(2)}) collective-permute-start(f32[2,4,1,2,128]{4,2,3,1,0:T(1,128)S(1)} %get-tuple-element.21), channel_id=1, source_target_pairs={{0,1},{1,0},{2,3},{3,2},{4,5},{5,4},{6,7},{7,6},{8,9},{9,8},{10,11... | collective-permute-start | bytes 24584 | tf_op jit(solution)/shard_map/ppermute | solution.py:87
  13.7 1.5 %collective-permute-done.3 = f32[2,4,1,2,128]{4,2,3,1,0:T(1,128)S(1)} collective-permute-done((f32[2,4,1,2,128]{4,2,3,1,0:T(1,128)S(1)}, f32[2,4,1,2,128]{4,2,3,1,0:T(1,128)S(1)}, u32[]{:S(2)}, u32[]{:S(2)}) %collective-permute-start.3) | collective-permute-done | bytes 8224 | tf_op jit(solution)/shard_map/ppermute | solution.py:87
  15.2 2.0 %collective-permute-done.4 = f32[2,4,1,2,128]{4,2,3,1,0:T(1,128)S(1)} collective-permute-done((f32[2,4,1,2,128]{4,2,3,1,0:T(1,128)S(1)}, f32[2,4,1,2,128]{4,2,3,1,0:T(1,128)S(1)}, u32[]{:S(2)}, u32[]{:S(2)}) %collective-permute-start.4) | collective-permute-done | bytes 8224 | tf_op jit(solution)/shard_map/ppermute | solution.py:88
  17.3 0.6 copy-done.5
  18.1 0.5 copy-done.6
  19.2 0.7 copy-done.7
  21.0 0.5 copy-done.3
  21.9 0.5 copy-done.4
  25.3 0.6 copy-done.2
  25.9 1.4 %fusion.12 = f32[2,4,128,32]{2,3,1,0:T(8,128)S(1)} fusion(f32[]{:T(128)S(6)} %add.380, f32[2,4,128]{2,1,0:T(4,128)S(1)} %get-tuple-element.30, f32[]{:T(128)S(6)} %sub.974, f32[2,4,128]{2,1,0:T(4,128)S(1)} %get-tuple-element.29, pred[128,128]{1,0:T(8,128)(4,1)S(1)} %iota_compare_fusion, f32[1,2,4,32,128]{4,3,2,1,0:T(8,128)S(1)} %copy-done.2), kind=kOutput, calls=%fused_computation.42 | convolution fusion | flops 52559872 | bytes 286728 | tf_op jit(solution)/shard_map/xycq,xypq->xycp/dot_general | solution.py:199
  27.4 3.5 %collective-permute-start.7 = (f32[2,1,4,32,128]{4,3,2,1,0:T(8,128)S(1)}, f32[2,1,4,32,128]{4,3,2,1,0:T(8,128)S(1)}, u32[]{:S(2)}, u32[]{:S(2)}) collective-permute-start(f32[2,1,4,32,128]{4,3,2,1,0:T(8,128)S(1)} %get-tuple-element.11), channel_id=1, source_target_pairs={{2,0},{4,2},{6,4},{8,6},{10,8},{12,10},{14,12},{0,14},{3,1},{5,3},... | collective-permute-start | bytes 393224 | tf_op jit(solution)/shard_map/ppermute | solution.py:88
  31.0 3.7 %collective-permute-done.6 = f32[2,1,4,32,128]{4,3,2,1,0:T(8,128)S(1)} collective-permute-done((f32[2,1,4,32,128]{4,3,2,1,0:T(8,128)S(1)}, f32[2,1,4,32,128]{4,3,2,1,0:T(8,128)S(1)}, u32[]{:S(2)}, u32[]{:S(2)}) %collective-permute-start.6) | collective-permute-done | bytes 131104 | tf_op jit(solution)/shard_map/ppermute | solution.py:87
  34.8 2.0 %collective-permute-start.8 = (f32[2,4,1,32,128]{4,3,2,1,0:T(8,128)S(1)}, f32[2,4,1,32,128]{4,3,2,1,0:T(8,128)S(1)}, u32[]{:S(2)}, u32[]{:S(2)}) collective-permute-start(f32[2,4,1,32,128]{4,3,2,1,0:T(8,128)S(1)} %get-tuple-element.7), channel_id=1, source_target_pairs={{0,1},{1,0},{2,3},{3,2},{4,5},{5,4},{6,7},{7,6},{8,9},{9,8},{10,11... | collective-permute-start | bytes 393224 | tf_op jit(solution)/shard_map/ppermute | solution.py:87
  36.8 0.9 fusion.31
  37.7 0.9 fusion.37
  38.6 0.8 convolution_add_fusion.3
  39.4 0.8 convolution_add_fusion.4
  40.2 1.1 %fusion.46 = f32[2,2,4,32,6]{3,4,2,1,0:T(8,128)S(1)} fusion(f32[128,6,1,1,1]{0,1,4,3,2:T(8,128)S(1)} %copy-done.18, f32[2,4,1,32,128]{4,3,2,1,0:T(8,128)S(1)} %collective-permute-done.9, f32[2,1,4,32,128]{4,3,2,1,0:T(8,128)S(1)} %collective-permute-done.7, f32[2,2,4,32,128]{4,3,2,1,0:T(8,128)S(1)} %constant_dynamic-update-slice_fusion.2, ...), kind=kOutput, calls=%fused_computation.92 | convolution fusion | flops 5210112 | bytes 670720 | tf_op jit(solution)/shard_map/...q,qk->...k/dot_general | solution.py:77
  42.5 1.1 %fusion.49 = f32[2,2,4,32,6]{3,4,2,1,0:T(8,128)S(1)} fusion(f32[128,6,1,1,1]{0,1,4,3,2:T(8,128)S(1)} %copy-done.17, f32[2,1,4,32,128]{4,3,2,1,0:T(8,128)S(1)} %collective-permute-done.7, f32[2,2,4,32,128]{4,3,2,1,0:T(8,128)S(1)} %constant_dynamic-update-slice_fusion.2, f32[2,1,4,32,128]{4,3,2,1,0:T(8,128)S(1)} %collective-permute-done.6, ...), kind=kOutput, calls=%fused_computation.95 | convolution fusion | flops 5210112 | bytes 670720 | tf_op jit(solution)/shard_map/...q,qk->...k/dot_general | solution.py:77
  44.8 1.1 %fusion.47 = f32[2,2,4,32,16]{3,4,2,1,0:T(8,128)S(1)} fusion(f32[128,16,1,1,1]{0,1,4,3,2:T(8,128)S(1)} %copy-done.14, f32[2,4,1,32,128]{4,3,2,1,0:T(8,128)S(1)} %collective-permute-done.9, f32[2,1,4,32,128]{4,3,2,1,0:T(8,128)S(1)} %collective-permute-done.7, f32[2,2,4,32,128]{4,3,2,1,0:T(8,128)S(1)} %constant_dynamic-update-slice_fusion.2, ...), kind=kOutput, calls=%fused_computation.93 | convolution fusion | flops 13074432 | bytes 696320 | tf_op jit(solution)/shard_map/...q,qk->...k/dot_general | solution.py:77
  47.1 1.1 %fusion.50 = f32[2,2,4,32,16]{3,4,2,1,0:T(8,128)S(1)} fusion(f32[128,16,1,1,1]{0,1,4,3,2:T(8,128)S(1)} %copy-done.13, f32[2,1,4,32,128]{4,3,2,1,0:T(8,128)S(1)} %collective-permute-done.7, f32[2,2,4,32,128]{4,3,2,1,0:T(8,128)S(1)} %constant_dynamic-update-slice_fusion.2, f32[2,1,4,32,128]{4,3,2,1,0:T(8,128)S(1)} %collective-permute-done.6, ...), kind=kOutput, calls=%fused_computation.96 | convolution fusion | flops 13074432 | bytes 696320 | tf_op jit(solution)/shard_map/...q,qk->...k/dot_general | solution.py:77
  49.4 1.1 %fusion.48 = f32[2,2,4,32,7]{3,4,2,1,0:T(8,128)S(1)} fusion(f32[128,7,1,1,1]{0,1,4,3,2:T(8,128)S(1)} %copy-done.16, f32[2,4,1,32,128]{4,3,2,1,0:T(8,128)S(1)} %collective-permute-done.9, f32[2,1,4,32,128]{4,3,2,1,0:T(8,128)S(1)} %collective-permute-done.7, f32[2,2,4,32,128]{4,3,2,1,0:T(8,128)S(1)} %constant_dynamic-update-slice_fusion.2, ...), kind=kOutput, calls=%fused_computation.94 | convolution fusion | flops 5996544 | bytes 673280 | tf_op jit(solution)/shard_map/...q,qk->...k/dot_general | solution.py:77
  51.7 1.1 %fusion.51 = f32[2,2,4,32,7]{3,4,2,1,0:T(8,128)S(1)} fusion(f32[128,7,1,1,1]{0,1,4,3,2:T(8,128)S(1)} %copy-done.15, f32[2,1,4,32,128]{4,3,2,1,0:T(8,128)S(1)} %collective-permute-done.7, f32[2,2,4,32,128]{4,3,2,1,0:T(8,128)S(1)} %constant_dynamic-update-slice_fusion.2, f32[2,1,4,32,128]{4,3,2,1,0:T(8,128)S(1)} %collective-permute-done.6, ...), kind=kOutput, calls=%fused_computation.97 | convolution fusion | flops 5996544 | bytes 673280 | tf_op jit(solution)/shard_map/...q,qk->...k/dot_general | solution.py:77
  54.2 0.5 copy-done.1
  55.8 1.6 %fusion.10 = f32[1,2,4,32,128]{4,3,2,1,0:T(8,128)S(1)} fusion(f32[1,2,4,32,128]{4,3,2,1,0:T(8,128)S(1)} %copy-done.11, f32[2,4,32,128]{3,2,1,0:T(8,128)S(1)} %fusion.397, f32[2,4,128,32]{2,3,1,0:T(8,128)S(1)} %fusion.12, f32[2,4,128]{2,1,0:T(4,128)S(1)} %get-tuple-element.28, f32[2,4,128]{2,1,0:T(4,128)S(1)} %get-tuple-element.26, ...), kind=kOutput, calls=%fused_computation.28 | convolution fusion | flops 53149696 | bytes 806912 | tf_op jit(solution)/shard_map/xycq,xypq->xycp/dot_general | solution.py:200
  57.4 1.8 %collective-permute-start.10 = (f32[1,2,4,32,128]{4,3,2,1,0:T(8,128)S(1)}, f32[1,2,4,32,128]{4,3,2,1,0:T(8,128)S(1)}, u32[]{:S(2)}, u32[]{:S(2)}) collective-permute-start(f32[1,2,4,32,128]{4,3,2,1,0:T(8,128)S(1)} %fusion.10), channel_id=1, source_target_pairs={{0,16},{16,0},{1,17},{17,1},{2,18},{18,2},{3,19},{19,3},{4,20},{20... | collective-permute-start | bytes 393224 | tf_op jit(solution)/shard_map/ppermute | solution.py:94
  59.2 3.5 %collective-permute-done.10 = f32[1,2,4,32,128]{4,3,2,1,0:T(8,128)S(1)} collective-permute-done((f32[1,2,4,32,128]{4,3,2,1,0:T(8,128)S(1)}, f32[1,2,4,32,128]{4,3,2,1,0:T(8,128)S(1)}, u32[]{:S(2)}, u32[]{:S(2)}) %collective-permute-start.10) | collective-permute-done | bytes 131104 | tf_op jit(solution)/shard_map/ppermute | solution.py:94
  62.7 3.5 %collective-permute-start.12 = (f32[2,1,4,32,128]{4,3,2,1,0:T(8,128)S(1)}, f32[2,1,4,32,128]{4,3,2,1,0:T(8,128)S(1)}, u32[]{:S(2)}, u32[]{:S(2)}) collective-permute-start(f32[2,1,4,32,128]{4,3,2,1,0:T(8,128)S(1)} %get-tuple-element.9), channel_id=1, source_target_pairs={{2,0},{4,2},{6,4},{8,6},{10,8},{12,10},{14,12},{0,14},{3,1},{5,3},... | collective-permute-start | bytes 393224 | tf_op jit(solution)/shard_map/ppermute | solution.py:88
  66.3 1.3 %fusion.11 = f32[2,4,32,128]{3,2,1,0:T(8,128)S(1)} fusion(f32[]{:T(128)S(6)} %add.380, f32[2,4,128]{2,1,0:T(4,128)S(1)} %get-tuple-element.30, f32[]{:T(128)S(6)} %sub.974, f32[2,4,128]{2,1,0:T(4,128)S(1)} %get-tuple-element.29, pred[128,128]{1,0:T(8,128)(4,1)S(1)} %iota_compare_fusion, f32[1,2,4,32,128]{4,3,2,1,0:T(8,128)S(1)} %fusion.10), kind=kOutput, calls=%fused_computation.41 | convolution fusion | flops 52559872 | bytes 286728 | tf_op jit(solution)/shard_map/xycq,xypq->xycp/dot_general | solution.py:199
  67.6 1.3 %collective-permute-done.11 = f32[2,1,4,32,128]{4,3,2,1,0:T(8,128)S(1)} collective-permute-done((f32[2,1,4,32,128]{4,3,2,1,0:T(8,128)S(1)}, f32[2,1,4,32,128]{4,3,2,1,0:T(8,128)S(1)}, u32[]{:S(2)}, u32[]{:S(2)}) %collective-permute-start.11) | collective-permute-done | bytes 131104 | tf_op jit(solution)/shard_map/ppermute | solution.py:87
  69.3 1.8 %collective-permute-start.13 = (f32[2,4,1,32,128]{4,3,2,1,0:T(8,128)S(1)}, f32[2,4,1,32,128]{4,3,2,1,0:T(8,128)S(1)}, u32[]{:S(2)}, u32[]{:S(2)}) collective-permute-start(f32[2,4,1,32,128]{4,3,2,1,0:T(8,128)S(1)} %get-tuple-element.5), channel_id=1, source_target_pairs={{0,1},{1,0},{2,3},{3,2},{4,5},{5,4},{6,7},{7,6},{8,9},{9,8},{10,11... | collective-permute-start | bytes 393224 | tf_op jit(solution)/shard_map/ppermute | solution.py:87
  71.0 0.9 fusion.15
  71.9 0.9 fusion.23
  72.8 0.8 convolution_add_fusion
  73.6 0.8 convolution_add_fusion.1
  74.4 1.1 %fusion.388 = f32[2,2,4,32,6]{3,4,2,1,0:T(8,128)S(1)} fusion(f32[128,6,1,1,1]{0,1,4,3,2:T(8,128)S(1)} %copy-done.18, f32[2,4,1,32,128]{4,3,2,1,0:T(8,128)S(1)} %collective-permute-done.14, f32[2,1,4,32,128]{4,3,2,1,0:T(8,128)S(1)} %collective-permute-done.12, f32[1,2,4,32,128]{4,3,2,1,0:T(8,128)S(1)} %collective-permute-done.10, ...), kind=kOutput, calls=%fused_computation.592 | convolution fusion | flops 5373952 | bytes 670720 | tf_op jit(solution)/shard_map/...q,qk->...k/dot_general | solution.py:77
  76.5 1.1 %fusion.391 = f32[2,2,4,32,6]{3,4,2,1,0:T(8,128)S(1)} fusion(f32[128,6,1,1,1]{0,1,4,3,2:T(8,128)S(1)} %copy-done.17, f32[2,1,4,32,128]{4,3,2,1,0:T(8,128)S(1)} %collective-permute-done.12, f32[1,2,4,32,128]{4,3,2,1,0:T(8,128)S(1)} %collective-permute-done.10, f32[1,2,4,32,128]{4,3,2,1,0:T(8,128)S(1)} %fusion.10, ...), kind=kOutput, calls=%fused_computation.595 | convolution fusion | flops 5373952 | bytes 670720 | tf_op jit(solution)/shard_map/...q,qk->...k/dot_general | solution.py:77
  78.6 1.1 %fusion.389 = f32[2,2,4,32,16]{3,4,2,1,0:T(8,128)S(1)} fusion(f32[128,16,1,1,1]{0,1,4,3,2:T(8,128)S(1)} %copy-done.14, f32[2,4,1,32,128]{4,3,2,1,0:T(8,128)S(1)} %collective-permute-done.14, f32[2,1,4,32,128]{4,3,2,1,0:T(8,128)S(1)} %collective-permute-done.12, f32[1,2,4,32,128]{4,3,2,1,0:T(8,128)S(1)} %collective-permute-done.10, ...), kind=kOutput, calls=%fused_computation.593 | convolution fusion | flops 13238272 | bytes 696320 | tf_op jit(solution)/shard_map/...q,qk->...k/dot_general | solution.py:77
  80.7 1.1 %fusion.392 = f32[2,2,4,32,16]{3,4,2,1,0:T(8,128)S(1)} fusion(f32[128,16,1,1,1]{0,1,4,3,2:T(8,128)S(1)} %copy-done.13, f32[2,1,4,32,128]{4,3,2,1,0:T(8,128)S(1)} %collective-permute-done.12, f32[1,2,4,32,128]{4,3,2,1,0:T(8,128)S(1)} %collective-permute-done.10, f32[1,2,4,32,128]{4,3,2,1,0:T(8,128)S(1)} %fusion.10, ...), kind=kOutput, calls=%fused_computation.596 | convolution fusion | flops 13238272 | bytes 696320 | tf_op jit(solution)/shard_map/...q,qk->...k/dot_general | solution.py:77
  82.8 1.1 %fusion.390 = f32[2,2,4,32,7]{3,4,2,1,0:T(8,128)S(1)} fusion(f32[128,7,1,1,1]{0,1,4,3,2:T(8,128)S(1)} %copy-done.16, f32[2,4,1,32,128]{4,3,2,1,0:T(8,128)S(1)} %collective-permute-done.14, f32[2,1,4,32,128]{4,3,2,1,0:T(8,128)S(1)} %collective-permute-done.12, f32[1,2,4,32,128]{4,3,2,1,0:T(8,128)S(1)} %collective-permute-done.10, ...), kind=kOutput, calls=%fused_computation.594 | convolution fusion | flops 6160384 | bytes 673280 | tf_op jit(solution)/shard_map/...q,qk->...k/dot_general | solution.py:77
  84.9 1.1 %fusion.393 = f32[2,2,4,32,7]{3,4,2,1,0:T(8,128)S(1)} fusion(f32[128,7,1,1,1]{0,1,4,3,2:T(8,128)S(1)} %copy-done.15, f32[2,1,4,32,128]{4,3,2,1,0:T(8,128)S(1)} %collective-permute-done.12, f32[1,2,4,32,128]{4,3,2,1,0:T(8,128)S(1)} %collective-permute-done.10, f32[1,2,4,32,128]{4,3,2,1,0:T(8,128)S(1)} %fusion.10, ...), kind=kOutput, calls=%fused_computation.597 | convolution fusion | flops 6160384 | bytes 673280 | tf_op jit(solution)/shard_map/...q,qk->...k/dot_general | solution.py:77
  87.7 2.2 %fusion.9 = f32[1,2,4,32,128]{4,3,2,1,0:T(8,128)} fusion(f32[1,2,4,32,128]{4,3,2,1,0:T(8,128)S(1)} %copy-done.2, f32[2,4,32,128]{3,2,1,0:T(8,128)S(1)} %fusion.398, f32[2,4,32,128]{3,2,1,0:T(8,128)S(1)} %fusion.11, f32[2,4,128]{2,1,0:T(4,128)S(1)} %get-tuple-element.28, f32[2,4,128]{2,1,0:T(4,128)S(1)} %get-tuple-element.26, ...), kind=kOutput, calls=%fused_computation.27 | convolution fusion | flops 53149696 | bytes 806912 | tf_op jit(solution)/shard_map/xycq,xypq->xycp/dot_general | solution.py:200
  (154 shorter events, 20.9 us)
Async XLA Ops:
  1.3 5.2 %collective-permute-start = (f32[1,2,4,2,128]{4,2,3,1,0:T(4,128)S(1)}, f32[1,2,4,2,128]{4,2,3,1,0:T(4,128)S(1)}, u32[]{:S(2)}, u32[]{:S(2)}) collective-permute-start(f32[1,2,4,2,128]{4,2,3,1,0:T(4,128)S(1)} %get-tuple-element.95), channel_id=1, source_target_pairs={{0,16},{16,0},{1,17},{17,1},{2,18},{18,2},{3,19},{19,3},{4,20},{20... | collective-permute-start | bytes 24584 | tf_op jit(solution)/shard_map/ppermute | solution.py:94
  4.3 23.0 %collective-permute-start.5 = (f32[1,2,4,32,128]{4,3,2,1,0:T(8,128)}, f32[1,2,4,32,128]{4,3,2,1,0:T(8,128)S(1)}, u32[]{:S(2)}, u32[]{:S(2)}) collective-permute-start(f32[1,2,4,32,128]{4,3,2,1,0:T(8,128)} %param.44), channel_id=1, source_target_pairs={{0,16},{16,0},{1,17},{17,1},{2,18},{18,2},{3,19},{19,3},{4,20},{20... | collective-permute-start | bytes 393224 | tf_op jit(solution)/shard_map/ppermute | solution.py:94
  5.6 0.7 copy-start.9
  5.6 0.7 copy-start.10
  6.5 4.9 %collective-permute-start.1 = (f32[2,1,4,2,128]{4,2,3,1,0:T(4,128)S(1)}, f32[2,1,4,2,128]{4,2,3,1,0:T(4,128)S(1)}, u32[]{:S(2)}, u32[]{:S(2)}) collective-permute-start(f32[2,1,4,2,128]{4,2,3,1,0:T(4,128)S(1)} %get-tuple-element.23), channel_id=1, source_target_pairs={{0,2},{2,4},{4,6},{6,8},{8,10},{10,12},{12,14},{14,0},{1,3},{3,5},... | collective-permute-start | bytes 24584 | tf_op jit(solution)/shard_map/ppermute | solution.py:87
  6.6 4.9 %collective-permute-start.2 = (f32[2,1,4,2,128]{4,2,3,1,0:T(4,128)S(1)}, f32[2,1,4,2,128]{4,2,3,1,0:T(4,128)S(1)}, u32[]{:S(2)}, u32[]{:S(2)}) collective-permute-start(f32[2,1,4,2,128]{4,2,3,1,0:T(4,128)S(1)} %get-tuple-element.24), channel_id=1, source_target_pairs={{2,0},{4,2},{6,4},{8,6},{10,8},{12,10},{14,12},{0,14},{3,1},{5,3},... | collective-permute-start | bytes 24584 | tf_op jit(solution)/shard_map/ppermute | solution.py:88
  11.5 3.7 %collective-permute-start.3 = (f32[2,4,1,2,128]{4,2,3,1,0:T(1,128)S(1)}, f32[2,4,1,2,128]{4,2,3,1,0:T(1,128)S(1)}, u32[]{:S(2)}, u32[]{:S(2)}) collective-permute-start(f32[2,4,1,2,128]{4,2,3,1,0:T(1,128)S(1)} %get-tuple-element.21), channel_id=1, source_target_pairs={{0,1},{1,0},{2,3},{3,2},{4,5},{5,4},{6,7},{7,6},{8,9},{9,8},{10,11... | collective-permute-start | bytes 24584 | tf_op jit(solution)/shard_map/ppermute | solution.py:87
  13.6 3.7 %collective-permute-start.4 = (f32[2,4,1,2,128]{4,2,3,1,0:T(1,128)S(1)}, f32[2,4,1,2,128]{4,2,3,1,0:T(1,128)S(1)}, u32[]{:S(2)}, u32[]{:S(2)}) collective-permute-start(f32[2,4,1,2,128]{4,2,3,1,0:T(1,128)S(1)} %get-tuple-element.22), channel_id=1, source_target_pairs={{1,0},{0,1},{3,2},{2,3},{5,4},{4,5},{7,6},{6,7},{9,8},{8,9},{11,10... | collective-permute-start | bytes 24584 | tf_op jit(solution)/shard_map/ppermute | solution.py:88
  17.2 0.7 copy-start.5
  17.9 0.7 copy-start.6
  19.1 0.7 copy-start.7
  20.0 0.7 copy-start.8
  20.8 0.7 copy-start.3
  21.7 0.7 copy-start.4
  25.0 0.9 %copy-start.2 = (f32[1,2,4,32,128]{4,3,2,1,0:T(8,128)S(1)}, f32[1,2,4,32,128]{4,3,2,1,0:T(8,128)}, u32[]{:S(2)}) copy-start(f32[1,2,4,32,128]{4,3,2,1,0:T(8,128)} %param.44) | copy-start | bytes 393220
  27.4 7.3 %collective-permute-start.6 = (f32[2,1,4,32,128]{4,3,2,1,0:T(8,128)S(1)}, f32[2,1,4,32,128]{4,3,2,1,0:T(8,128)S(1)}, u32[]{:S(2)}, u32[]{:S(2)}) collective-permute-start(f32[2,1,4,32,128]{4,3,2,1,0:T(8,128)S(1)} %get-tuple-element.10), channel_id=1, source_target_pairs={{0,2},{2,4},{4,6},{6,8},{8,10},{10,12},{12,14},{14,0},{1,3},{3,5},... | collective-permute-start | bytes 393224 | tf_op jit(solution)/shard_map/ppermute | solution.py:87
  27.4 7.3 %collective-permute-start.7 = (f32[2,1,4,32,128]{4,3,2,1,0:T(8,128)S(1)}, f32[2,1,4,32,128]{4,3,2,1,0:T(8,128)S(1)}, u32[]{:S(2)}, u32[]{:S(2)}) collective-permute-start(f32[2,1,4,32,128]{4,3,2,1,0:T(8,128)S(1)} %get-tuple-element.11), channel_id=1, source_target_pairs={{2,0},{4,2},{6,4},{8,6},{10,8},{12,10},{14,12},{0,14},{3,1},{5,3},... | collective-permute-start | bytes 393224 | tf_op jit(solution)/shard_map/ppermute | solution.py:88
  34.7 5.5 %collective-permute-start.9 = (f32[2,4,1,32,128]{4,3,2,1,0:T(8,128)S(1)}, f32[2,4,1,32,128]{4,3,2,1,0:T(8,128)S(1)}, u32[]{:S(2)}, u32[]{:S(2)}) collective-permute-start(f32[2,4,1,32,128]{4,3,2,1,0:T(8,128)S(1)} %get-tuple-element.6), channel_id=1, source_target_pairs={{1,0},{0,1},{3,2},{2,3},{5,4},{4,5},{7,6},{6,7},{9,8},{8,9},{11,10... | collective-permute-start | bytes 393224 | tf_op jit(solution)/shard_map/ppermute | solution.py:88
  34.8 7.5 %collective-permute-start.8 = (f32[2,4,1,32,128]{4,3,2,1,0:T(8,128)S(1)}, f32[2,4,1,32,128]{4,3,2,1,0:T(8,128)S(1)}, u32[]{:S(2)}, u32[]{:S(2)}) collective-permute-start(f32[2,4,1,32,128]{4,3,2,1,0:T(8,128)S(1)} %get-tuple-element.7), channel_id=1, source_target_pairs={{0,1},{1,0},{2,3},{3,2},{4,5},{5,4},{6,7},{7,6},{8,9},{9,8},{10,11... | collective-permute-start | bytes 393224 | tf_op jit(solution)/shard_map/ppermute | solution.py:87
  39.4 0.8 copy-start.18
  41.8 0.7 copy-start.17
  44.1 0.7 copy-start.14
  46.4 0.7 copy-start.13
  48.8 0.7 copy-start.16
  51.0 0.7 copy-start.15
  53.8 0.9 copy-start.1
  54.7 0.9 %copy-start.11 = (f32[1,2,4,32,128]{4,3,2,1,0:T(8,128)S(1)}, f32[1,2,4,32,128]{4,3,2,1,0:T(8,128)}, u32[]{:S(2)}) copy-start(f32[1,2,4,32,128]{4,3,2,1,0:T(8,128)} %param.43) | copy-start | bytes 393220
  55.1 0.7 copy-start.12
  57.4 30.3 %copy-start = (f32[1,2,4,32,128]{4,3,2,1,0:T(8,128)}, f32[1,2,4,32,128]{4,3,2,1,0:T(8,128)S(1)}, u32[]{:S(2)}) copy-start(f32[1,2,4,32,128]{4,3,2,1,0:T(8,128)S(1)} %fusion.10) | copy-start | bytes 393220
  57.4 5.3 %collective-permute-start.10 = (f32[1,2,4,32,128]{4,3,2,1,0:T(8,128)S(1)}, f32[1,2,4,32,128]{4,3,2,1,0:T(8,128)S(1)}, u32[]{:S(2)}, u32[]{:S(2)}) collective-permute-start(f32[1,2,4,32,128]{4,3,2,1,0:T(8,128)S(1)} %fusion.10), channel_id=1, source_target_pairs={{0,16},{16,0},{1,17},{17,1},{2,18},{18,2},{3,19},{19,3},{4,20},{20... | collective-permute-start | bytes 393224 | tf_op jit(solution)/shard_map/ppermute | solution.py:94
  62.7 6.2 %collective-permute-start.11 = (f32[2,1,4,32,128]{4,3,2,1,0:T(8,128)S(1)}, f32[2,1,4,32,128]{4,3,2,1,0:T(8,128)S(1)}, u32[]{:S(2)}, u32[]{:S(2)}) collective-permute-start(f32[2,1,4,32,128]{4,3,2,1,0:T(8,128)S(1)} %get-tuple-element.8), channel_id=1, source_target_pairs={{0,2},{2,4},{4,6},{6,8},{8,10},{10,12},{12,14},{14,0},{1,3},{3,5},... | collective-permute-start | bytes 393224 | tf_op jit(solution)/shard_map/ppermute | solution.py:87
  62.7 6.2 %collective-permute-start.12 = (f32[2,1,4,32,128]{4,3,2,1,0:T(8,128)S(1)}, f32[2,1,4,32,128]{4,3,2,1,0:T(8,128)S(1)}, u32[]{:S(2)}, u32[]{:S(2)}) collective-permute-start(f32[2,1,4,32,128]{4,3,2,1,0:T(8,128)S(1)} %get-tuple-element.9), channel_id=1, source_target_pairs={{2,0},{4,2},{6,4},{8,6},{10,8},{12,10},{14,12},{0,14},{3,1},{5,3},... | collective-permute-start | bytes 393224 | tf_op jit(solution)/shard_map/ppermute | solution.py:88
  68.9 5.5 %collective-permute-start.14 = (f32[2,4,1,32,128]{4,3,2,1,0:T(8,128)S(1)}, f32[2,4,1,32,128]{4,3,2,1,0:T(8,128)S(1)}, u32[]{:S(2)}, u32[]{:S(2)}) collective-permute-start(f32[2,4,1,32,128]{4,3,2,1,0:T(8,128)S(1)} %get-tuple-element.4), channel_id=1, source_target_pairs={{1,0},{0,1},{3,2},{2,3},{5,4},{4,5},{7,6},{6,7},{9,8},{8,9},{11,10... | collective-permute-start | bytes 393224 | tf_op jit(solution)/shard_map/ppermute | solution.py:88
  69.3 7.2 %collective-permute-start.13 = (f32[2,4,1,32,128]{4,3,2,1,0:T(8,128)S(1)}, f32[2,4,1,32,128]{4,3,2,1,0:T(8,128)S(1)}, u32[]{:S(2)}, u32[]{:S(2)}) collective-permute-start(f32[2,4,1,32,128]{4,3,2,1,0:T(8,128)S(1)} %get-tuple-element.5), channel_id=1, source_target_pairs={{0,1},{1,0},{2,3},{3,2},{4,5},{5,4},{6,7},{7,6},{8,9},{9,8},{10,11... | collective-permute-start | bytes 393224 | tf_op jit(solution)/shard_map/ppermute | solution.py:87
where the time goes:
time: 90.5 us; the launch traced here: 89.8 us
  matrix products  42.7 us (47%)
  starting transfers between devices  21.9 us (24%)
  waiting for transfers between devices  13.4 us (15%)
  local copies, waits for them, and re-layouts  9.69 us (11%)
  between operations  1.41 us (2%)
    dot_general x36, matrix products, pick(): return jnp.einsum('...q,qk->...k', x, _one_hot(idx), precision=HI)  17.3 us
    dot_general x18, matrix products, hop_terms(): jnp.einsum('xycq,xypq->xycp', near[1], inter, precision=HI)  13 us
    dot_general x18, matrix products, hop_terms(): summed = jnp.einsum('xycq,xypq->xycp', near[0], plane, precision=HI)  11.6 us
    ppermute x6, starting transfers between devices, extended_2(): after = lax.ppermute(first, axis, down)  11.1 us
    unnamed x40, local copies, waits for them, and re-layouts  8.57 us
    ppermute x6, waiting for transfers between devices, extended_2(): before = lax.ppermute(last, axis, up)  7.9 us
    ppermute x6, starting transfers between devices, extended_2(): before = lax.ppermute(last, axis, up)  6.04 us
    ppermute x3, starting transfers between devices, partner_2(): lax.ppermute(value, axis, [(i, i ^ 1 << distance) for i in range(lax.axis...  4.77 us
  transfers between devices with their start and end apart: 15, of which 6 were waited for; matrix products, arithmetic and copies ran while one was open for 22% of the time, Pallas kernels for 0%

commit v1 on v0

--- a/solution.py
+++ b/solution.py
@@ -84,8 +84,13 @@
         down = [(j, i) for i, j in up]
         last = lax.slice_in_dim(value, length - width, length, axis=dim)
         first = lax.slice_in_dim(value, 0, width, axis=dim)
-        before = lax.ppermute(last, axis, up)
-        after = lax.ppermute(first, axis, down)
+        if devices == 2:
+            both = lax.ppermute(jnp.concatenate([last, first], axis=dim), axis, up)
+            before = lax.slice_in_dim(both, 0, width, axis=dim)
+            after = lax.slice_in_dim(both, width, 2 * width, axis=dim)
+        else:
+            before = lax.ppermute(last, axis, up)
+            after = lax.ppermute(first, axis, down)
         value = jnp.concatenate([before, value, after], axis=dim)
     return value
 
@@ -139,14 +144,20 @@
     return bonds * taper(dist_sq)
 
 
+def exchange(value):
+    stacked = jnp.concatenate([value, partner_2(value, "layer", 0)], axis=0)
+    return extended_2(stacked, (("gx", 1), ("gy", 2)), 1)
+
+
 def body(prev_vec, cur_vec, displace, potential):
     layer_id = lax.axis_index("layer")
     tile_x = displace.shape[1]
     tile_y = displace.shape[2]
     cos_twist = math.cos(twist_angle)
     sin_twist = math.sin(twist_angle)
-    partner = partner_2(displace, "layer", 0)
-    both_disp = jnp.concatenate([displace, partner], axis=0)
+    packed = exchange(jnp.concatenate([cur_vec, displace], axis=-2))
+    vec_ext = packed[..., : cur_vec.shape[-2], :]
+    ext_disp = packed[..., cur_vec.shape[-2] :, :]
     layer_up = layer_id == 1
     cos_vals = jnp.stack(
         [jnp.where(layer_up, cos_twist, 1.0), jnp.where(layer_up, 1.0, cos_twist)]
@@ -154,7 +165,6 @@
     sin_vals = jnp.stack(
         [jnp.where(layer_up, sin_twist, 0.0), jnp.where(layer_up, 0.0, sin_twist)]
     ).astype(jnp.float32)
-    ext_disp = extended_2(both_disp, (("gx", 1), ("gy", 2)), 1)
     places = ext_disp + lattice(cos_vals, sin_vals)[:, None, None]
     row_count = tile_x * lax.axis_size("gx")
     col_count = tile_y * lax.axis_size("gy")
@@ -164,51 +174,60 @@
     col_ids = (
         lax.axis_index("gy") * tile_y + jnp.arange(tile_y + 2, dtype=jnp.int32) - 1 + col_count
     ) % col_count
-    twisted = places + twist_offsets(cos_vals, sin_vals, row_ids, col_ids)
+    turn = twist_offsets(cos_vals, sin_vals, row_ids, col_ids)
+    twisted = places + turn
 
     def own_view(value, a, b):
         return value[:, 1 + a : 1 + a + tile_x, 1 + b : 1 + b + tile_y]
 
     own_pos = own_view(places[:1], 0, 0)[0]
-    own_twist = own_view(twisted[:1], 0, 0)[0]
+    own_shift = own_view(turn[:1], 0, 0)[0]
     cos_own = cos_vals[0]
     sin_own = sin_vals[0]
-    blocks = []
+    narrow = [o for o in OFFSETS if len(REACH[o][0]) < 64]
+    narrow_rows = np.concatenate([REACH[o][0] for o in narrow])
+    picked = jnp.einsum("...q,qk->...k", own_pos, _one_hot(narrow_rows), precision=HI)
+    blocks = {}
+    columns = {}
+    at = 0
     for a, b in OFFSETS:
         rows, cols = REACH[(a, b)]
+        if len(rows) < 64:
+            own_rows = picked[..., at : at + len(rows)]
+            at += len(rows)
+            cols = np.arange(128)
+        else:
+            own_rows = pick(own_pos, rows)
         shift_x = cos_own * (a * cell_w) - sin_own * (b * cell_h)
         shift_y = sin_own * (a * cell_w) + cos_own * (b * cell_h)
         near_pos = pick(own_view(places[:1], a, b)[0], cols)
         near_twist = pick(own_view(twisted[1:], a, b)[0], cols)
-        plane = plane_block(pick(own_pos, rows), near_pos, shift_x, shift_y, a == 0 and b == 0)
-        inter = inter_block(pick(own_twist, rows), near_twist, a * cell_w, b * cell_h)
-        blocks.append((plane, inter))
-
-    spread_rows = np.concatenate([REACH[o][0] for o in OFFSETS if len(REACH[o][0]) < 128])
-    scatter = np.zeros((len(spread_rows), 128), np.float32)
-    scatter[np.arange(len(spread_rows)), spread_rows] = 1.0
-
-    def hop_terms(vectors):
-        stacked = jnp.concatenate([vectors, partner_2(vectors, "layer", 0)], axis=0)
-        extended = extended_2(stacked, (("gx", 1), ("gy", 2)), 1)
+        plane = plane_block(own_rows, near_pos, shift_x, shift_y, a == 0 and b == 0)
+        inter = inter_block(own_rows + own_shift, near_twist, a * cell_w, b * cell_h)
+        blocks[(a, b)] = (plane, inter)
+        columns[(a, b)] = cols
+    blocks = lax.optimization_barrier(blocks)
+
+    scatter = np.zeros((len(narrow_rows), 128), np.float32)
+    scatter[np.arange(len(narrow_rows)), narrow_rows] = 1.0
+
+    def hop_terms(vectors, extended):
         full = potential[0][..., None, :] * vectors[0]
-        parts = []
-        for (a, b), (plane, inter) in zip(OFFSETS, blocks):
-            rows, cols = REACH[(a, b)]
-            near = pick(own_view(extended, a, b), cols)
+        parts = {}
+        for a, b in OFFSETS:
+            plane, inter = blocks[(a, b)]
+            near = pick(own_view(extended, a, b), columns[(a, b)])
             summed = jnp.einsum("xycq,xypq->xycp", near[0], plane, precision=HI)
-            summed = summed + jnp.einsum("xycq,xypq->xycp", near[1], inter, precision=HI)
-            if len(rows) == 128:
-                full = full + summed
-            else:
-                parts.append(summed)
+            parts[(a, b)] = summed + jnp.einsum("xycq,xypq->xycp", near[1], inter, precision=HI)
+        full = full + parts[(0, 0)]
+        full = full + jnp.concatenate([parts[(-1, 0)], parts[(1, 0)]], axis=-1)
         full = full + jnp.einsum(
-            "xycp,pn->xycn", jnp.concatenate(parts, axis=-1), scatter, precision=HI
+            "xycp,pn->xycn", jnp.concatenate([parts[o] for o in narrow], axis=-1), scatter, precision=HI
         )
         return (full / hop_scale)[None]
 
-    first_term = 2.0 * hop_terms(cur_vec) - prev_vec
-    second_term = 2.0 * hop_terms(first_term) - cur_vec
+    first_term = 2.0 * hop_terms(cur_vec, vec_ext) - prev_vec
+    second_term = 2.0 * hop_terms(first_term, exchange(first_term)) - cur_vec
     return (first_term, second_term)
 
 

time: 90.5 us -> 72.6 us (0.80)
  matrix products: 42.7 us -> 17.6 us
  waiting for transfers between devices: 13.4 us -> 24.7 us
  starting transfers between devices: 21.9 us -> 10.8 us
  other arithmetic: 0.69 us -> 7.64 us
    dot_general x38 -> x3, matrix products: 18.1 us -> 1.61 us  [the longest x2 1.43 us: hop_terms(): jnp.einsum('xycp,pn->xycn', jnp.concatenate([parts[o] for o in narrow], a...]
    ppermute x6 -> x2, starting transfers between devices: 11.1 us -> 2.75 us  [extended_2(): after = lax.ppermute(first, axis, down)]
    ppermute x0 -> x2, waiting for transfers between devices: none -> 6.65 us  [extended_2(): both = lax.ppermute(jnp.concatenate([last, first], axis=dim), axis, up)]
    ppermute x6 -> x2, starting transfers between devices: 6.04 us -> 0.3 us  [extended_2(): before = lax.ppermute(last, axis, up)]
    dot_general x18, matrix products: 13 us -> 8.32 us  [hop_terms(): jnp.einsum('xycq,xypq->xycp', near[1], inter, precision=HI)]
    dot_general x18, matrix products: 11.6 us -> 7.65 us  [hop_terms(): summed = jnp.einsum('xycq,xypq->xycp', near[0], plane, precision=HI)]
    mul x0 -> x17, other arithmetic: none -> 3.31 us  [the longest x9 2.02 us: inter_block(): return bonds * taper(dist_sq)]
    ppermute x6 -> x2, waiting for transfers between devices: 2.07 us -> 5.27 us  [extended_2(): after = lax.ppermute(first, axis, down)]
  transfers between devices with their start and end apart: 15 -> 8, of which waited for: 6 -> 8; matrix products, arithmetic and copies ran while one was open for 22% -> 6% of each run, Pallas kernels for 0% -> 0%
where the time goes in v1:
time: 72.6 us; the launch traced here: 71.9 us
  waiting for transfers between devices  24.7 us (34%)
  matrix products  17.6 us (24%)
  starting transfers between devices  10.8 us (15%)
  local copies, waits for them, and re-layouts  9.7 us (13%)
  other arithmetic  7.64 us (11%)
  between operations  1.49 us (2%)
    dot_general x18, matrix products, hop_terms(): jnp.einsum('xycq,xypq->xycp', near[1], inter, precision=HI)  8.32 us
    dot_general x18, matrix products, hop_terms(): summed = jnp.einsum('xycq,xypq->xycp', near[0], plane, precision=HI)  7.65 us
    ppermute x2, waiting for transfers between devices, extended_2(): before = lax.ppermute(last, axis, up)  6.82 us
    unnamed x49, local copies, waits for them, and re-layouts  6.71 us
    ppermute x2, waiting for transfers between devices, extended_2(): both = lax.ppermute(jnp.concatenate([last, first], axis=dim), axis, up)  6.65 us
    ppermute x2, waiting for transfers between devices, partner_2(): lax.ppermute(value, axis, [(i, i ^ 1 << distance) for i in range(lax.axis...  5.96 us
    ppermute x2, waiting for transfers between devices, extended_2(): after = lax.ppermute(first, axis, down)  5.27 us
    ppermute x2, starting transfers between devices, partner_2(): lax.ppermute(value, axis, [(i, i ^ 1 << distance) for i in range(lax.axis...  4.6 us
  transfers between devices with their start and end apart: 8, of which 8 were waited for; matrix products, arithmetic and copies ran while one was open for 6% of the time, Pallas kernels for 0%

profile of v1, /device:TPU:0, one launch (start us, length us, event | category | flops | bytes accessed | tf_op | source)
XLA Modules:
  0.0 71.9 jit_solution(1121604180146311943)
XLA Ops:
  0.6 1.0 %copy_dynamic-update-slice_fusion = f32[1,2,4,34,128]{4,2,3,1,0:T(4,128)S(1)} fusion(f32[1,2,4,32,128]{4,3,2,1,0:T(8,128)} %param.9), kind=kLoop, calls=%fused_computation.159 | loop fusion | bytes 262144
  1.7 3.0 %collective-permute-start = (f32[1,2,4,34,128]{4,2,3,1,0:T(4,128)S(1)}, f32[1,2,4,34,128]{4,2,3,1,0:T(4,128)S(1)}, u32[]{:S(2)}, u32[]{:S(2)}) collective-permute-start(f32[1,2,4,34,128]{4,2,3,1,0:T(4,128)S(1)} %copy_dynamic-update-slice_fusion.1), channel_id=1, source_target_pairs={{0,16},{16,0},{1,17},{17,1},{2,18},{18,2},{3,19},{19,3},{4,20},{20... | collective-permute-start | bytes 417800 | tf_op jit(solution)/shard_map/ppermute | solution.py:99
  5.1 0.7 copy-done.22
  5.9 2.5 %collective-permute-done = f32[1,2,4,34,128]{4,2,3,1,0:T(4,128)S(1)} collective-permute-done((f32[1,2,4,34,128]{4,2,3,1,0:T(4,128)S(1)}, f32[1,2,4,34,128]{4,2,3,1,0:T(4,128)S(1)}, u32[]{:S(2)}, u32[]{:S(2)}) %collective-permute-start) | collective-permute-done | bytes 139296 | tf_op jit(solution)/shard_map/ppermute | solution.py:99
  8.4 2.5 %collective-permute-start.2 = (f32[2,1,4,34,128]{4,2,3,1,0:T(4,128)S(1)}, f32[2,1,4,34,128]{4,2,3,1,0:T(4,128)S(1)}, u32[]{:S(2)}, u32[]{:S(2)}) collective-permute-start(f32[2,1,4,34,128]{4,2,3,1,0:T(4,128)S(1)} %get-tuple-element.67), channel_id=1, source_target_pairs={{2,0},{4,2},{6,4},{8,6},{10,8},{12,10},{14,12},{0,14},{3,1},{5,3},... | collective-permute-start | bytes 417800 | tf_op jit(solution)/shard_map/ppermute | solution.py:93
  10.9 3.0 %collective-permute-done.2 = f32[2,1,4,34,128]{4,2,3,1,0:T(4,128)S(1)} collective-permute-done((f32[2,1,4,34,128]{4,2,3,1,0:T(4,128)S(1)}, f32[2,1,4,34,128]{4,2,3,1,0:T(4,128)S(1)}, u32[]{:S(2)}, u32[]{:S(2)}) %collective-permute-start.2) | collective-permute-done | bytes 139296 | tf_op jit(solution)/shard_map/ppermute | solution.py:93
  13.9 3.3 %collective-permute-done.1 = f32[2,1,4,34,128]{4,2,3,1,0:T(4,128)S(1)} collective-permute-done((f32[2,1,4,34,128]{4,2,3,1,0:T(4,128)S(1)}, f32[2,1,4,34,128]{4,2,3,1,0:T(4,128)S(1)}, u32[]{:S(2)}, u32[]{:S(2)}) %collective-permute-start.1) | collective-permute-done | bytes 139296 | tf_op jit(solution)/shard_map/ppermute | solution.py:92
  17.5 1.6 %collective-permute-start.3 = (f32[2,4,2,34,128]{4,2,3,1,0:T(2,128)S(1)}, f32[2,4,2,34,128]{4,2,3,1,0:T(2,128)S(1)}, u32[]{:S(2)}, u32[]{:S(2)}) collective-permute-start(f32[2,4,2,34,128]{4,2,3,1,0:T(2,128)S(1)} %fusion.12), channel_id=1, source_target_pairs={{0,1},{1,0},{2,3},{3,2},{4,5},{5,4},{6,7},{7,6},{8,9},{9,8},{10,11... | collective-permute-start | bytes 835592 | tf_op jit(solution)/shard_map/ppermute | solution.py:88
  19.2 0.9 %maximum_bitcast_fusion.15 = (f32[2,4,32,64]{3,1,2,0:T(4,128)S(1)}, f32[2,4,32,64]{3,1,2,0:T(4,128)}, f32[2,4,32,64]{3,1,2,0:T(4,128)}, f32[2,4,32,64]{3,1,2,0:T(4,128)S(1)}) fusion(f32[2,1,4,34,128]{4,2,3,1,0:T(4,128)S(1)} %collective-permute-done.1, f32[1,2,4,34,128]{4,2,3,1,0:T(4,128)S(1)} %collective-permute-done, ...), kind=kLoop, calls=%fused_computation.126 | loop fusion | flops 131072 | bytes 819200 | tf_op jit(solution)/shard_map/squeeze | solution.py:220
  20.1 4.0 %collective-permute-done.3 = f32[2,4,2,34,128]{4,2,3,1,0:T(2,128)S(1)} collective-permute-done((f32[2,4,2,34,128]{4,2,3,1,0:T(2,128)S(1)}, f32[2,4,2,34,128]{4,2,3,1,0:T(2,128)S(1)}, u32[]{:S(2)}, u32[]{:S(2)}) %collective-permute-start.3) | collective-permute-done | bytes 278560 | tf_op jit(solution)/shard_map/ppermute | solution.py:88
  24.5 0.7 copy-done.19
  26.5 0.3 maximum_multiply_fusion.3
  27.2 0.6 maximum_multiply_fusion
  28.0 0.3 maximum_multiply_fusion.1
  28.5 0.5 multiply_select_fusion
  29.1 0.3 maximum_multiply_fusion.4
  30.4 0.5 copy-done.1
  30.9 1.6 %convolution_bitcast_fusion = f32[2,4,32,128]{3,2,1,0:T(8,128)} fusion(f32[2,4,128,128]{3,2,1,0:T(8,128)S(1)} %multiply_select_fusion, f32[1,2,4,32,128]{4,3,2,1,0:T(8,128)S(1)} %copy-done.1), kind=kOutput, calls=%fused_computation.10 | convolution fusion | flops 50331648 | bytes 786432 | tf_op jit(solution)/shard_map/xycq,xypq->xycp/dot_general | solution.py:220
  33.8 0.8 %fusion.38 = (f32[2,4,32,128]{3,1,2,0:T(4,128)S(1)}, f32[2,4,32,128]{3,1,2,0:T(4,128)S(1)}, f32[2,4,32,128]{3,1,2,0:T(4,128)S(1)}, f32[2,4,32,128]{3,1,2,0:T(4,128)}) fusion(f32[2,4,1,34,128]{4,2,3,1,0:T(1,128)S(1)} %get-tuple-element.65, f32[2,1,4,34,128]{4,2,3,1,0:T(4,128)S(1)} %collective-permute-done.2, ...), kind=kLoop, calls=%fused_computation.100 | loop fusion | flops 393216 | bytes 1351680 | tf_op jit(solution)/shard_map/squeeze | solution.py:221
  36.8 0.9 %convolution_add_fusion.12 = f32[2,4,32,7]{3,2,1,0:T(8,128)} fusion(f32[2,4,32,7]{3,2,1,0:T(8,128)S(1)} %fusion.47, f32[2,4,7,128]{3,2,1,0:T(8,128)S(1)} %maximum_multiply_fusion.9, f32[2,4,32,128]{3,1,2,0:T(4,128)S(1)} %get-tuple-element.44), kind=kOutput, calls=%fused_computation.23 | convolution fusion | flops 2754304 | bytes 174080 | tf_op jit(solution)/shard_map/xycq,xypq->xycp/dot_general | solution.py:221
  37.7 1.8 %concatenate.91 = f32[2,4,32,58]{3,2,1,0:T(8,128)} concatenate(f32[2,4,32,6]{3,2,1,0:T(8,128)S(1)} %convolution_add_fusion.17, f32[2,4,32,6]{3,2,1,0:T(8,128)S(1)} %convolution_add_fusion.16, f32[2,4,32,16]{3,2,1,0:T(8,128)S(1)} %convolution_add_fusion.15, f32[2,4,32,16]{3,2,1,0:T(8,128)S(1)} %convolution_add_fusion.14, f32[2,4,32,7]{3,2,1,0:T(8,128)S(1)} %convolution_add_fusion.13, ...), dimensions={3} | concatenate | bytes 118784 | tf_op jit(solution)/shard_map/concatenate | solution.py:225
  39.5 1.2 %fusion.92 = f32[2,4,32,128]{3,2,1,0:T(8,128)S(1)} fusion(f32[2,4,32,58]{3,2,1,0:T(8,128)} %concatenate.91, f32[58,128,1,1]{1,0,3,2:T(8,128)S(1)} %copy-done.17), kind=kOutput, calls=%fused_computation.323 | convolution fusion | flops 22806528 | bytes 220160 | tf_op jit(solution)/shard_map/xycp,pn->xycn/dot_general | solution.py:224
  40.8 0.5 fusion.64
  41.3 0.4 copy-done.2
  41.7 0.5 fusion.67
  42.2 0.5 convolution_add_fusion.3
  42.7 0.5 convolution_add_fusion.4
  43.3 0.3 copy-done.4
  43.7 0.9 %fusion.11 = f32[1,2,4,32,128]{4,3,2,1,0:T(8,128)S(1)} fusion(f32[1,2,4,32,128]{4,3,2,1,0:T(8,128)S(1)} %copy-done.16, f32[2,4,32,128]{3,2,1,0:T(8,128)S(1)} %fusion.92, f32[2,4,32,128]{3,2,1,0:T(8,128)S(1)} %copy-done.4, f32[2,4,128,128]{3,2,1,0:T(8,128)S(1)} %maximum_multiply_fusion, f32[2,4,32,64]{3,2,1,0:T(8,128)S(1)} %convolution_add_fusion.3, ...), kind=kOutput, calls=%fused_computation.30 | convolution fusion | flops 50593792 | bytes 1445888 | tf_op jit(solution)/shard_map/xycq,xypq->xycp/dot_general | solution.py:221
  44.7 1.6 %collective-permute-start.4 = (f32[1,2,4,32,128]{4,3,2,1,0:T(8,128)S(1)}, f32[1,2,4,32,128]{4,3,2,1,0:T(8,128)S(1)}, u32[]{:S(2)}, u32[]{:S(2)}) collective-permute-start(f32[1,2,4,32,128]{4,3,2,1,0:T(8,128)S(1)} %fusion.11), channel_id=1, source_target_pairs={{0,16},{16,0},{1,17},{17,1},{2,18},{18,2},{3,19},{19,3},{4,20},{20... | collective-permute-start | bytes 393224 | tf_op jit(solution)/shard_map/ppermute | solution.py:99
  46.3 3.5 %collective-permute-done.4 = f32[1,2,4,32,128]{4,3,2,1,0:T(8,128)S(1)} collective-permute-done((f32[1,2,4,32,128]{4,3,2,1,0:T(8,128)S(1)}, f32[1,2,4,32,128]{4,3,2,1,0:T(8,128)S(1)}, u32[]{:S(2)}, u32[]{:S(2)}) %collective-permute-start.4) | collective-permute-done | bytes 131104 | tf_op jit(solution)/shard_map/ppermute | solution.py:99
  50.0 0.3 collective-permute-start.5
  50.3 0.9 %fusion.43 = f32[2,4,32,128]{3,2,1,0:T(8,128)S(1)} fusion(f32[2,4,128,128]{3,2,1,0:T(8,128)S(1)} %multiply_select_fusion, f32[1,2,4,32,128]{4,3,2,1,0:T(8,128)S(1)} %fusion.11), kind=kOutput, calls=%fused_computation.129 | convolution fusion | flops 50331648 | bytes 786432 | tf_op jit(solution)/shard_map/xycq,xypq->xycp/dot_general | solution.py:220
  51.2 2.3 %collective-permute-done.6 = f32[2,1,4,32,128]{4,3,2,1,0:T(8,128)S(1)} collective-permute-done((f32[2,1,4,32,128]{4,3,2,1,0:T(8,128)S(1)}, f32[2,1,4,32,128]{4,3,2,1,0:T(8,128)S(1)}, u32[]{:S(2)}, u32[]{:S(2)}) %collective-permute-start.6) | collective-permute-done | bytes 131104 | tf_op jit(solution)/shard_map/ppermute | solution.py:93
  53.5 3.5 %collective-permute-done.5 = f32[2,1,4,32,128]{4,3,2,1,0:T(8,128)S(1)} collective-permute-done((f32[2,1,4,32,128]{4,3,2,1,0:T(8,128)S(1)}, f32[2,1,4,32,128]{4,3,2,1,0:T(8,128)S(1)}, u32[]{:S(2)}, u32[]{:S(2)}) %collective-permute-start.5) | collective-permute-done | bytes 131104 | tf_op jit(solution)/shard_map/ppermute | solution.py:92
  57.1 1.6 %collective-permute-start.7 = (f32[2,4,2,32,128]{4,3,2,1,0:T(8,128)S(1)}, f32[2,4,2,32,128]{4,3,2,1,0:T(8,128)S(1)}, u32[]{:S(2)}, u32[]{:S(2)}) collective-permute-start(f32[2,4,2,32,128]{4,3,2,1,0:T(8,128)S(1)} %fusion.13), channel_id=1, source_target_pairs={{0,1},{1,0},{2,3},{3,2},{4,5},{5,4},{6,7},{7,6},{8,9},{9,8},{10,11... | collective-permute-start | bytes 786440 | tf_op jit(solution)/shard_map/ppermute | solution.py:88
  58.7 0.5 fusion.23
  59.2 0.5 convolution_add_fusion
  59.7 0.6 fusion.31
  60.3 0.6 convolution_add_fusion.1
  60.9 2.6 %collective-permute-done.7 = f32[2,4,2,32,128]{4,3,2,1,0:T(8,128)S(1)} collective-permute-done((f32[2,4,2,32,128]{4,3,2,1,0:T(8,128)S(1)}, f32[2,4,2,32,128]{4,3,2,1,0:T(8,128)S(1)}, u32[]{:S(2)}, u32[]{:S(2)}) %collective-permute-start.7) | collective-permute-done | bytes 262176 | tf_op jit(solution)/shard_map/ppermute | solution.py:88
  65.0 0.5 copy-done.7
  65.8 0.5 copy-done.9
  66.5 0.5 copy-done.11
  67.8 0.5 copy-done.13
  68.5 0.5 copy-done.15
  69.6 0.5 copy-done.18
  70.3 1.6 %fusion.10 = f32[1,2,4,32,128]{4,3,2,1,0:T(8,128)} fusion(f32[1,2,4,32,128]{4,3,2,1,0:T(8,128)S(1)} %copy-done.1, f32[2,4,32,128]{3,2,1,0:T(8,128)S(1)} %fusion.93, f32[2,4,32,128]{3,2,1,0:T(8,128)S(1)} %fusion.43, f32[2,4,128,128]{3,2,1,0:T(8,128)S(1)} %maximum_multiply_fusion, f32[2,4,32,64]{3,2,1,0:T(8,128)S(1)} %convolution_add_fusion, ...), kind=kOutput, calls=%fused_computation.29 | convolution fusion | flops 50593792 | bytes 1445888 | tf_op jit(solution)/shard_map/xycq,xypq->xycp/dot_general | solution.py:221
  (144 shorter events, 11.6 us)
Async XLA Ops:
  0.6 1.0 %copy-start.21 = (f32[1,2,4,2,128]{4,3,2,1,0:T(2,128)S(1)}, f32[1,2,4,2,128]{4,3,2,1,0:T(2,128)}, u32[]{:S(2)}) copy-start(f32[1,2,4,2,128]{4,3,2,1,0:T(2,128)} %param.10) | copy-start | bytes 24580
  1.7 6.7 %collective-permute-start = (f32[1,2,4,34,128]{4,2,3,1,0:T(4,128)S(1)}, f32[1,2,4,34,128]{4,2,3,1,0:T(4,128)S(1)}, u32[]{:S(2)}, u32[]{:S(2)}) collective-permute-start(f32[1,2,4,34,128]{4,2,3,1,0:T(4,128)S(1)} %copy_dynamic-update-slice_fusion.1), channel_id=1, source_target_pairs={{0,16},{16,0},{1,17},{17,1},{2,18},{18,2},{3,19},{19,3},{4,20},{20... | collective-permute-start | bytes 417800 | tf_op jit(solution)/shard_map/ppermute | solution.py:99
  5.1 0.7 copy-start.22
  5.1 0.7 copy-start.23
  8.4 5.5 %collective-permute-start.2 = (f32[2,1,4,34,128]{4,2,3,1,0:T(4,128)S(1)}, f32[2,1,4,34,128]{4,2,3,1,0:T(4,128)S(1)}, u32[]{:S(2)}, u32[]{:S(2)}) collective-permute-start(f32[2,1,4,34,128]{4,2,3,1,0:T(4,128)S(1)} %get-tuple-element.67), channel_id=1, source_target_pairs={{2,0},{4,2},{6,4},{8,6},{10,8},{12,10},{14,12},{0,14},{3,1},{5,3},... | collective-permute-start | bytes 417800 | tf_op jit(solution)/shard_map/ppermute | solution.py:93
  10.9 6.3 %collective-permute-start.1 = (f32[2,1,4,34,128]{4,2,3,1,0:T(4,128)S(1)}, f32[2,1,4,34,128]{4,2,3,1,0:T(4,128)S(1)}, u32[]{:S(2)}, u32[]{:S(2)}) collective-permute-start(f32[2,1,4,34,128]{4,2,3,1,0:T(4,128)S(1)} %get-tuple-element.66), channel_id=1, source_target_pairs={{0,2},{2,4},{4,6},{6,8},{8,10},{10,12},{12,14},{14,0},{1,3},{3,5},... | collective-permute-start | bytes 417800 | tf_op jit(solution)/shard_map/ppermute | solution.py:92
  17.5 6.6 %collective-permute-start.3 = (f32[2,4,2,34,128]{4,2,3,1,0:T(2,128)S(1)}, f32[2,4,2,34,128]{4,2,3,1,0:T(2,128)S(1)}, u32[]{:S(2)}, u32[]{:S(2)}) collective-permute-start(f32[2,4,2,34,128]{4,2,3,1,0:T(2,128)S(1)} %fusion.12), channel_id=1, source_target_pairs={{0,1},{1,0},{2,3},{3,2},{4,5},{5,4},{6,7},{7,6},{8,9},{9,8},{10,11... | collective-permute-start | bytes 835592 | tf_op jit(solution)/shard_map/ppermute | solution.py:88
  24.4 0.8 %copy-start.19 = (f32[128,58,1,1]{0,1,3,2:T(8,128)S(1)}, f32[128,58,1,1]{0,1,3,2:T(8,128)}, u32[]{:S(2)}) copy-start(f32[128,58,1,1]{0,1,3,2:T(8,128)} %constant.239) | copy-start | bytes 89092
  26.5 8.9 %copy-start.8 = (f32[2,4,6,128]{3,2,1,0:T(8,128)}, f32[2,4,6,128]{3,2,1,0:T(8,128)S(1)}, u32[]{:S(2)}) copy-start(f32[2,4,6,128]{3,2,1,0:T(8,128)S(1)} %maximum_multiply_fusion.15) | copy-start | bytes 73732
  27.0 8.7 %copy-start.10 = (f32[2,4,6,128]{3,2,1,0:T(8,128)}, f32[2,4,6,128]{3,2,1,0:T(8,128)S(1)}, u32[]{:S(2)}) copy-start(f32[2,4,6,128]{3,2,1,0:T(8,128)S(1)} %maximum_multiply_fusion.13) | copy-start | bytes 73732
  28.0 8.5 %copy-start.12 = (f32[2,4,7,128]{3,2,1,0:T(8,128)}, f32[2,4,7,128]{3,2,1,0:T(8,128)S(1)}, u32[]{:S(2)}) copy-start(f32[2,4,7,128]{3,2,1,0:T(8,128)S(1)} %maximum_multiply_fusion.11) | copy-start | bytes 86020
  28.5 8.3 %copy-start.14 = (f32[2,4,7,128]{3,2,1,0:T(8,128)}, f32[2,4,7,128]{3,2,1,0:T(8,128)S(1)}, u32[]{:S(2)}) copy-start(f32[2,4,7,128]{3,2,1,0:T(8,128)S(1)} %maximum_multiply_fusion.9) | copy-start | bytes 86020
  30.0 0.9 %copy-start.1 = (f32[1,2,4,32,128]{4,3,2,1,0:T(8,128)S(1)}, f32[1,2,4,32,128]{4,3,2,1,0:T(8,128)}, u32[]{:S(2)}) copy-start(f32[1,2,4,32,128]{4,3,2,1,0:T(8,128)} %param.9) | copy-start | bytes 393220
  30.9 4.3 %copy-start.6 = (f32[2,4,7,128]{3,2,1,0:T(8,128)}, f32[2,4,7,128]{3,2,1,0:T(8,128)S(1)}, u32[]{:S(2)}) copy-start(f32[2,4,7,128]{3,2,1,0:T(8,128)S(1)} %maximum_multiply_fusion.10) | copy-start | bytes 86020
  37.7 1.8 %copy-start.17 = (f32[58,128,1,1]{1,0,3,2:T(8,128)S(1)}, f32[58,128,1,1]{1,0,3,2:T(8,128)}, u32[]{:S(2)}) copy-start(f32[58,128,1,1]{1,0,3,2:T(8,128)} %constant.240) | copy-start | bytes 89092
  39.5 1.2 %copy-start.3 = (f32[2,4,32,64]{3,1,2,0:T(4,128)S(1)}, f32[2,4,32,64]{3,1,2,0:T(4,128)}, u32[]{:S(2)}) copy-start(f32[2,4,32,64]{3,1,2,0:T(4,128)} %get-tuple-element.62) | copy-start | bytes 196612
  40.7 0.9 %copy-start.2 = (f32[2,4,32,64]{3,1,2,0:T(4,128)S(1)}, f32[2,4,32,64]{3,1,2,0:T(4,128)}, u32[]{:S(2)}) copy-start(f32[2,4,32,64]{3,1,2,0:T(4,128)} %get-tuple-element.59) | copy-start | bytes 196612
  42.7 0.9 %copy-start.4 = (f32[2,4,32,128]{3,2,1,0:T(8,128)S(1)}, f32[2,4,32,128]{3,2,1,0:T(8,128)}, u32[]{:S(2)}) copy-start(f32[2,4,32,128]{3,2,1,0:T(8,128)} %convolution_bitcast_fusion) | copy-start | bytes 393220
  42.7 1.0 %copy-start.5 = (f32[2,4,32,128]{3,1,2,0:T(4,128)S(1)}, f32[2,4,32,128]{3,1,2,0:T(4,128)}, u32[]{:S(2)}) copy-start(f32[2,4,32,128]{3,1,2,0:T(4,128)} %get-tuple-element.72) | copy-start | bytes 393220
  42.7 1.0 %copy-start.16 = (f32[1,2,4,32,128]{4,3,2,1,0:T(8,128)S(1)}, f32[1,2,4,32,128]{4,3,2,1,0:T(8,128)}, u32[]{:S(2)}) copy-start(f32[1,2,4,32,128]{4,3,2,1,0:T(8,128)} %param.8) | copy-start | bytes 393220
  42.7 1.0 %copy-start.20 = (f32[1,2,4,128]{3,2,1,0:T(4,128)S(1)}, f32[1,2,4,128]{3,2,1,0:T(4,128)}, u32[]{:S(2)}) copy-start(f32[1,2,4,128]{3,2,1,0:T(4,128)} %param.11) | copy-start | bytes 12292
  44.7 25.6 %copy-start = (f32[1,2,4,32,128]{4,3,2,1,0:T(8,128)}, f32[1,2,4,32,128]{4,3,2,1,0:T(8,128)S(1)}, u32[]{:S(2)}) copy-start(f32[1,2,4,32,128]{4,3,2,1,0:T(8,128)S(1)} %fusion.11) | copy-start | bytes 393220
  44.7 5.0 %collective-permute-start.4 = (f32[1,2,4,32,128]{4,3,2,1,0:T(8,128)S(1)}, f32[1,2,4,32,128]{4,3,2,1,0:T(8,128)S(1)}, u32[]{:S(2)}, u32[]{:S(2)}) collective-permute-start(f32[1,2,4,32,128]{4,3,2,1,0:T(8,128)S(1)} %fusion.11), channel_id=1, source_target_pairs={{0,16},{16,0},{1,17},{17,1},{2,18},{18,2},{3,19},{19,3},{4,20},{20... | collective-permute-start | bytes 393224 | tf_op jit(solution)/shard_map/ppermute | solution.py:99
  49.8 3.8 %collective-permute-start.6 = (f32[2,1,4,32,128]{4,3,2,1,0:T(8,128)S(1)}, f32[2,1,4,32,128]{4,3,2,1,0:T(8,128)S(1)}, u32[]{:S(2)}, u32[]{:S(2)}) collective-permute-start(f32[2,1,4,32,128]{4,3,2,1,0:T(8,128)S(1)} %get-tuple-element.71), channel_id=1, source_target_pairs={{2,0},{4,2},{6,4},{8,6},{10,8},{12,10},{14,12},{0,14},{3,1},{5,3},... | collective-permute-start | bytes 393224 | tf_op jit(solution)/shard_map/ppermute | solution.py:93
  50.0 7.0 %collective-permute-start.5 = (f32[2,1,4,32,128]{4,3,2,1,0:T(8,128)S(1)}, f32[2,1,4,32,128]{4,3,2,1,0:T(8,128)S(1)}, u32[]{:S(2)}, u32[]{:S(2)}) collective-permute-start(f32[2,1,4,32,128]{4,3,2,1,0:T(8,128)S(1)} %get-tuple-element.70), channel_id=1, source_target_pairs={{0,2},{2,4},{4,6},{6,8},{8,10},{10,12},{12,14},{14,0},{1,3},{3,5},... | collective-permute-start | bytes 393224 | tf_op jit(solution)/shard_map/ppermute | solution.py:92
  57.1 6.4 %collective-permute-start.7 = (f32[2,4,2,32,128]{4,3,2,1,0:T(8,128)S(1)}, f32[2,4,2,32,128]{4,3,2,1,0:T(8,128)S(1)}, u32[]{:S(2)}, u32[]{:S(2)}) collective-permute-start(f32[2,4,2,32,128]{4,3,2,1,0:T(8,128)S(1)} %fusion.13), channel_id=1, source_target_pairs={{0,1},{1,0},{2,3},{3,2},{4,5},{5,4},{6,7},{7,6},{8,9},{9,8},{10,11... | collective-permute-start | bytes 786440 | tf_op jit(solution)/shard_map/ppermute | solution.py:88
  64.7 0.8 %copy-start.7 = (f32[2,4,7,128]{3,2,1,0:T(8,128)S(1)}, f32[2,4,7,128]{3,2,1,0:T(8,128)}, u32[]{:S(2)}) copy-start(f32[2,4,7,128]{3,2,1,0:T(8,128)} %copy-done.6) | copy-start | bytes 86020
  65.5 0.8 %copy-start.9 = (f32[2,4,6,128]{3,2,1,0:T(8,128)S(1)}, f32[2,4,6,128]{3,2,1,0:T(8,128)}, u32[]{:S(2)}) copy-start(f32[2,4,6,128]{3,2,1,0:T(8,128)} %copy-done.8) | copy-start | bytes 73732
  66.3 0.8 %copy-start.11 = (f32[2,4,6,128]{3,2,1,0:T(8,128)S(1)}, f32[2,4,6,128]{3,2,1,0:T(8,128)}, u32[]{:S(2)}) copy-start(f32[2,4,6,128]{3,2,1,0:T(8,128)} %copy-done.10) | copy-start | bytes 73732
  67.5 0.8 %copy-start.13 = (f32[2,4,7,128]{3,2,1,0:T(8,128)S(1)}, f32[2,4,7,128]{3,2,1,0:T(8,128)}, u32[]{:S(2)}) copy-start(f32[2,4,7,128]{3,2,1,0:T(8,128)} %copy-done.12) | copy-start | bytes 86020
  68.3 0.8 %copy-start.15 = (f32[2,4,7,128]{3,2,1,0:T(8,128)S(1)}, f32[2,4,7,128]{3,2,1,0:T(8,128)}, u32[]{:S(2)}) copy-start(f32[2,4,7,128]{3,2,1,0:T(8,128)} %copy-done.14) | copy-start | bytes 86020
  69.3 0.8 %copy-start.18 = (f32[58,128,1,1]{1,0,3,2:T(8,128)S(1)}, f32[58,128,1,1]{1,0,3,2:T(8,128)}, u32[]{:S(2)}) copy-start(f32[58,128,1,1]{1,0,3,2:T(8,128)} %constant.240) | copy-start | bytes 89092
